TPU v7x, 32 devices: a whole 2x2x4 slice. The times are simulated.
32 devices in a mesh: seq: 8 (over y, x, core), head: 4 (over z).
Axes of the slice: x: 2, y: 2, z: 4, core: 2. Of those that a mesh axis runs over, the one named last changes fastest.
Arguments:
- tokens: bfloat16 [4096, 5376], P('seq', 'head'), may hold values from -32 to 32
- query_weight: bfloat16 [5376, 4096], P(None, 'head'), may hold values from -1 to 1
- key_weight: bfloat16 [5376, 2048], P(None, 'head'), may hold values from -1 to 1
- value_weight: bfloat16 [5376, 2048], P(None, 'head'), may hold values from -0.078125 to 0.078125
- output_grad: bfloat16 [4096, 4096], P('seq', 'head'), may hold values from -48 to 48
- segments: int32 [4096], replicated, may hold values from 0 to 3, never falling along the last dimension, each value on 1 to 2048 neighbouring positions
Outputs:
- token_grad: bfloat16 [4096, 5376], P('seq', 'head')
- query_weight_grad: bfloat16 [5376, 4096], P('seq', 'head')
- key_weight_grad: bfloat16 [5376, 2048], P('seq', 'head')
- value_weight_grad: bfloat16 [5376, 2048], P('seq', 'head')
Inputs may be any that keep to these rules, and one draw needn't show every extreme that they name: `segments`: segment numbers never fall along the tokens; a segment has at most 2048 tokens.
All inputs are finite; a program needn't handle non-finite values.
Results may differ from a plain program's by a relative error of at most 0.015.
The roundings to bfloat16 on the way count: a program that leaves them out, or rounds other values in their place, can miss the bound.
Values may be sent and summed in bfloat16 or wider, within the bound.
No kernel may reach another device: no remote copies, remote signals or barrier semaphores. Data moves between devices by JAX's collectives and lax.ppermute only.
A program may use at most 192 MiB of HBM per device.

v0:
```python
import jax
import jax.numpy as jnp
from jax import lax
from jax.sharding import Mesh, PartitionSpec as P

D = 5376
HEADS = 32
KV_HEADS = 16
HEAD_DIM = 128
WINDOW = 1024
HOPS = 2
SEQ = ("seq_hi", "core")
neg_large = -1e30


def passed_along(x, axis, by):
    count = lax.axis_size(axis)
    pairs = [(i, i + by) for i in range(count) if 0 <= i + by < count]
    return lax.ppermute(x, axis, pairs)


def contract_last(left, right):
    return lax.dot_general(
        left, right, (((1,), (1,)), ((), ())), preferred_element_type=jnp.float32
    )


def contract_first(left, right):
    return lax.dot_general(
        left, right, (((0,), (0,)), ((), ())), preferred_element_type=jnp.float32
    )


def attend(queries, key_value, grads, query_first, key_first, seg_query, seg_key):
    tok_rows = queries.shape[0]
    key_rows = key_value.shape[1]
    groups = HEADS // KV_HEADS
    kv_local = key_value.shape[2] // HEAD_DIM
    score_scale = (D / HEADS) ** (-0.5)
    query_four = queries.reshape(tok_rows, kv_local, groups, HEAD_DIM)
    grad_four = grads.reshape(tok_rows, kv_local, groups, HEAD_DIM)
    key_three = key_value[0].reshape(key_rows, kv_local, HEAD_DIM)
    value_three = key_value[1].reshape(key_rows, kv_local, HEAD_DIM)
    query_pos = query_first + jnp.arange(tok_rows, dtype=jnp.int32)
    key_pos = key_first + jnp.arange(key_rows, dtype=jnp.int32)
    spacing = query_pos[:, None] - key_pos[None, :]
    allowed = (
        (key_pos >= 0)[None, :]
        & (spacing >= 0)
        & (spacing < WINDOW)
        & (seg_query[:, None] == seg_key[None, :])
    )
    scores = (
        jnp.einsum("akgd,ckd->kgac", query_four, key_three, preferred_element_type=jnp.float32)
        * score_scale
    )
    masked = jnp.where(allowed, scores, neg_large)
    row_max = jnp.max(masked, axis=-1, keepdims=True)
    expo = jnp.where(allowed, jnp.exp(masked - row_max), 0.0)
    probs = expo / jnp.sum(expo, axis=-1, keepdims=True)
    dprobs = jnp.einsum(
        "akgd,ckd->kgac", grad_four, value_three, preferred_element_type=jnp.float32
    )
    center = jnp.sum(probs * dprobs, axis=-1, keepdims=True)
    dscores = (probs * (dprobs - center)).astype(jnp.bfloat16)
    probs_low = probs.astype(jnp.bfloat16)
    query_grad = (
        (
            jnp.einsum("kgac,ckd->akgd", dscores, key_three, preferred_element_type=jnp.float32)
            * score_scale
        )
        .reshape(tok_rows, -1)
        .astype(jnp.bfloat16)
    )
    key_grad = (
        jnp.einsum("kgac,akgd->ckd", dscores, query_four, preferred_element_type=jnp.float32)
        * score_scale
    ).reshape(key_rows, -1)
    value_grad = jnp.einsum(
        "kgac,akgd->ckd", probs_low, grad_four, preferred_element_type=jnp.float32
    ).reshape(key_rows, -1)
    return (query_grad, jnp.stack([key_grad, value_grad]))


def per_device(tokens, query_weight, key_weight, value_weight, output_grad, segments):
    tok_rows = tokens.shape[0]
    hop_count = HOPS
    margin = hop_count * tok_rows
    gathered = lax.all_gather(tokens, "head", axis=1, tiled=True)
    queries = jnp.dot(gathered, query_weight, preferred_element_type=jnp.float32).astype(
        jnp.bfloat16
    )
    keys_own = jnp.dot(gathered, key_weight, preferred_element_type=jnp.float32).astype(
        jnp.bfloat16
    )
    values_own = jnp.dot(gathered, value_weight, preferred_element_type=jnp.float32).astype(
        jnp.bfloat16
    )
    key_value = jnp.stack([keys_own, values_own])
    blocks = [key_value] * (hop_count + 1)
    for distance in range(1, hop_count + 1):
        blocks[hop_count - distance] = passed_along(key_value, SEQ, distance)
    keys_all = jnp.concatenate(blocks, axis=1)
    position = lax.axis_index(SEQ)
    query_first = position * tok_rows
    seg_query = lax.dynamic_slice_in_dim(segments, query_first, tok_rows, 0)
    seg_padded = jnp.concatenate([jnp.full((margin,), -1, jnp.int32), segments], axis=0)
    seg_key = lax.dynamic_slice_in_dim(seg_padded, query_first, (hop_count + 1) * tok_rows, 0)
    query_grad, kv_grad = attend(
        queries, keys_all, output_grad, query_first, query_first - margin, seg_query, seg_key
    )
    pieces = [
        kv_grad[:, block * tok_rows : (block + 1) * tok_rows] for block in range(hop_count + 1)
    ]
    carried = pieces[hop_count]
    for distance in range(1, hop_count + 1):
        back = passed_along(pieces[hop_count - distance].astype(jnp.bfloat16), SEQ, -distance)
        carried = carried + back.astype(jnp.float32)
    key_grad = carried[0].astype(jnp.bfloat16)
    value_grad = carried[1].astype(jnp.bfloat16)
    n_head = lax.axis_size("head")
    me = lax.axis_index("head")
    width = tokens.shape[1]

    def term(dest):
        start = dest * width
        part = contract_last(query_grad, lax.dynamic_slice_in_dim(query_weight, start, width, 0))
        part = part + contract_last(key_grad, lax.dynamic_slice_in_dim(key_weight, start, width, 0))
        part = part + contract_last(
            value_grad, lax.dynamic_slice_in_dim(value_weight, start, width, 0)
        )
        return part.astype(jnp.bfloat16)

    token_sum = None
    for shift in range(n_head - 1, 0, -1):
        sent = term((me + shift) % n_head)
        pairs = [(i, (i + shift) % n_head) for i in range(n_head)]
        got = lax.ppermute(sent, "head", pairs).astype(jnp.float32)
        token_sum = got if token_sum is None else token_sum + got
    own = term(me).astype(jnp.float32)
    token_grad = (own if token_sum is None else token_sum + own).astype(jnp.bfloat16)
    proj_grads = jnp.concatenate([query_grad, key_grad, value_grad], axis=1)
    weight_part = contract_first(proj_grads, gathered).astype(jnp.bfloat16)
    n_seq = lax.axis_size(SEQ)
    block = weight_part.shape[1] // n_seq

    def weight_block(dest):
        return lax.dynamic_slice_in_dim(weight_part, dest * block, block, 1)

    weight_sum = weight_block(position).astype(jnp.float32)
    for shift in range(n_seq - 1, 0, -1):
        sent = weight_block((position + shift) % n_seq)
        pairs = [(i, (i + shift) % n_seq) for i in range(n_seq)]
        weight_sum = weight_sum + lax.ppermute(sent, SEQ, pairs).astype(jnp.float32)
    summed = (weight_sum * (tok_rows * n_seq) ** (-0.5)).astype(jnp.bfloat16).T
    q_width = query_weight.shape[1]
    k_width = key_weight.shape[1]
    query_weight_grad = summed[:, :q_width]
    key_weight_grad = summed[:, q_width : q_width + k_width]
    value_weight_grad = summed[:, q_width + k_width :]
    return (token_grad, query_weight_grad, key_weight_grad, value_weight_grad)


def solution(mesh):
    n_seq = mesh.shape["seq"]
    n_head = mesh.shape["head"]
    view = Mesh(mesh.devices.reshape(n_seq // 2, 2, n_head), ("seq_hi", "core", "head"))
    in_specs = (
        P(SEQ, "head"),
        P(None, "head"),
        P(None, "head"),
        P(None, "head"),
        P(SEQ, "head"),
        P(),
    )
    out_specs = (P(SEQ, "head"),) * 4
    return jax.shard_map(
        per_device, mesh=view, in_specs=in_specs, out_specs=out_specs, check_vma=False
    )
```

profile of v0, /device:TPU:27, one launch (start us, length us, event | category | flops | bytes accessed | tf_op | source)
XLA Modules:
  0.0 638.8 jit_solution(9430814455776416603)
XLA Ops:
  10.5 2.6 fusion.16
  13.1 97.3 %all-gather.2.cloned.1.call-done = bf16[512,5376]{0,1:T(8,128)(2,1)} async-done(((bf16[512,1344]{0,1:T(8,128)(2,1)}), bf16[512,5376]{0,1:T(8,128)(2,1)}) %all-gather.2.cloned.1.call-update) | async-done | bytes 5505040 | tf_op jit(solution)/shard_map/all_gather | solution.py:89
  110.5 7.3 %fusion.53 = bf16[1,512,512]{2,1,0:T(8,128)(2,1)S(1)} fusion(bf16[512,5376]{0,1:T(8,128)(2,1)} %all-gather.2.cloned.1.call-done, bf16[5376,512]{1,0:T(8,128)(2,1)} %param.9), kind=kOutput, calls=%fused_computation.77 | convolution fusion | flops 2818834432 | bytes 11534336 | tf_op jit(solution)/shard_map/dot_general | solution.py:96
  117.9 5.7 fusion.52
  123.7 3.4 collective-permute-start.1
  127.2 3.1 collective-permute-start
  130.3 5.9 convolution_convert_fusion.1
  138.1 9.5 %collective-permute-done.1 = bf16[2,512,512]{2,1,0:T(8,128)(2,1)} collective-permute-done((bf16[2,512,512]{2,1,0:T(8,128)(2,1)S(1)}, bf16[2,512,512]{2,1,0:T(8,128)(2,1)}, u32[]{:S(2)}, u32[]{:S(2)}) %collective-permute-start.1) | collective-permute-done | bytes 1048608 | tf_op jit(solution)/shard_map/ppermute | solution.py:19
  147.5 14.7 %collective-permute-done = bf16[2,512,512]{2,1,0:T(8,128)(2,1)} collective-permute-done((bf16[2,512,512]{2,1,0:T(8,128)(2,1)S(1)}, bf16[2,512,512]{2,1,0:T(8,128)(2,1)}, u32[]{:S(2)}, u32[]{:S(2)}) %collective-permute-start) | collective-permute-done | bytes 1048608 | tf_op jit(solution)/shard_map/ppermute | solution.py:19
  166.7 4.0 reshape_squeeze.7
  170.8 13.6 %fusion.72 = (f32[4,2,512]{2,1,0:T(2,128)S(1)}, f32[4,2,512,1536]{2,3,1,0:T(8,128)}) fusion(pred[512,1536]{0,1:T(8,128)(4,1)S(1)} %copy-done.11, bf16[1536,4,128,1]{0,2,3,1:T(8,128)(2,1)S(1)} %copy.63, bf16[512,4,2,128]{0,3,2,1:T(8,128)(2,1)S(1)} %bitcast.81), kind=kOutput, calls=%fused_computation.110 | convolution fusion | flops 1642071552 | bytes 28590080 | tf_op jit(solution)/shard_map/sub | solution.py:59
  184.3 17.5 %fusion.1 = (f32[4,2,512]{2,1,0:T(2,128)S(1)}, f32[4,1536,512,2]{2,1,3,0:T(8,128)}) fusion(f32[4,2,512,1536]{2,3,1,0:T(8,128)} %get-tuple-element.28, f32[4,2,512]{2,1,0:T(2,128)S(1)} %get-tuple-element.27, bf16[512,4,2,128]{0,3,2,1:T(8,128)(2,1)} %bitcast.83, bf16[1536,4,128,1]{2,1,0,3:T(4,128)(2,1)} %bitcast.82), kind=kOutput, calls=%fused_computation.3 | convolution fusion | flops 1629483008 | bytes 52985856 | tf_op jit(solution)/shard_map/akgd,ckd->kgac/dot_general | solution.py:61
  201.9 17.0 %fusion.3 = bf16[4,2,512,1536]{2,3,1,0:T(8,128)(2,1)S(1)} fusion(f32[4,1536,512,2]{2,1,3,0:T(8,128)} %get-tuple-element.30, f32[4,2,512]{2,1,0:T(2,128)S(1)} %get-tuple-element.29, f32[4,2,512,1536]{2,3,1,0:T(8,128)} %get-tuple-element.28, f32[4,2,512]{2,1,0:T(2,128)S(1)} %get-tuple-element.27), kind=kLoop, calls=%fused_computation.5 | loop fusion | flops 25165824 | bytes 62947328 | tf_op jit(solution)/shard_map/convert_element_type | solution.py:65
  218.9 2.8 multiply_convert_fusion.1
  221.7 7.0 %fusion.13 = f32[4,128,1536]{2,1,0:T(8,128)} fusion(bf16[512,4,2,128]{0,3,2,1:T(8,128)(2,1)} %bitcast.80, bf16[4,2,512,1536]{2,3,1,0:T(8,128)(2,1)S(1)} %fusion.3), kind=kOutput, calls=%fused_computation.33 | convolution fusion | flops 1611399168 | bytes 16777216 | tf_op jit(solution)/shard_map/kgac,akgd->ckd/dot_general | solution.py:76
  228.7 11.0 %fusion.5 = f32[4,1536,128,1]{1,2,3,0:T(8,128)S(1)} fusion(bf16[512,4,2,128]{0,3,2,1:T(8,128)(2,1)} %bitcast.84, f32[4,2,512,1536]{2,3,1,0:T(8,128)} %get-tuple-element.28, f32[4,2,512]{2,1,0:T(2,128)S(1)} %get-tuple-element.27), kind=kOutput, calls=%fused_computation.10 | convolution fusion | flops 1623195648 | bytes 29376512 | tf_op jit(solution)/shard_map/kgac,akgd->ckd/dot_general | solution.py:79
  244.7 3.5 fusion.25
  248.2 3.2 fusion.27
  251.4 3.2 fusion.29
  254.7 13.9 %collective-permute-done.3 = bf16[2,512,512]{1,2,0:T(8,128)(2,1)S(1)} collective-permute-done((bf16[2,512,512]{1,2,0:T(8,128)(2,1)S(1)}, bf16[2,512,512]{1,2,0:T(8,128)(2,1)S(1)}, u32[]{:S(2)}, u32[]{:S(2)}) %collective-permute-start.3) | collective-permute-done | bytes 1048608 | tf_op jit(solution)/shard_map/ppermute | solution.py:19
  268.5 3.7 collective-permute-done.2
  275.9 3.3 fusion.19
  279.3 2.9 collective-permute-start.6
  282.1 19.3 %convolution_convert_fusion = bf16[2048,5376]{0,1:T(8,128)(2,1)} fusion(bf16[512,5376]{0,1:T(8,128)(2,1)} %all-gather.2.cloned.1.call-done, bf16[512,512]{0,1:T(8,128)(2,1)} %get-tuple-element.26, bf16[512,512]{0,1:T(8,128)(2,1)} %get-tuple-element.25, bf16[512,1024]{0,1:T(8,128)(2,1)S(1)} %bitcast.88), kind=kOutput, calls=%fused_computation.8 | convolution fusion | flops 11291590656 | bytes 29622272 | tf_op jit(solution)/shard_map/dot_general | solution.py:29
  301.4 12.4 %constant_dynamic-slice_fusion.6 = (bf16[2048,672]{0,1:T(8,128)(2,1)}, bf16[2048,672]{0,1:T(8,128)(2,1)S(1)}, bf16[2048,672]{0,1:T(8,128)(2,1)S(1)}, bf16[2048,6...) fusion(bf16[2048,5376]{0,1:T(8,128)(2,1)} %convolution_convert_fusion, ...), kind=kLoop, calls=%fused_computation.89 | loop fusion | bytes 38535196 | tf_op jit(solution)/shard_map/dynamic_slice | solution.py:148
  324.9 85.2 %collective-permute-done.5 = bf16[512,1344]{0,1:T(8,128)(2,1)S(1)} collective-permute-done((bf16[512,1344]{0,1:T(8,128)(2,1)S(1)}, bf16[512,1344]{0,1:T(8,128)(2,1)S(1)}, u32[]{:S(2)}, u32[]{:S(2)}) %collective-permute-start.5) | collective-permute-done | bytes 1376288 | tf_op jit(solution)/shard_map/ppermute | solution.py:138
  413.5 16.9 %collective-permute-done.12 = bf16[2048,672]{0,1:T(8,128)(2,1)} collective-permute-done((bf16[2048,672]{0,1:T(8,128)(2,1)S(1)}, bf16[2048,672]{0,1:T(8,128)(2,1)}, u32[]{:S(2)}, u32[]{:S(2)}) %collective-permute-start.12) | collective-permute-done | bytes 2752544 | tf_op jit(solution)/shard_map/ppermute | solution.py:154
  430.6 3.4 fusion.23
  436.5 3.7 add_convert_fusion
  440.2 149.0 %collective-permute-done.10 = bf16[2048,672]{0,1:T(8,128)(2,1)} collective-permute-done((bf16[2048,672]{0,1:T(8,128)(2,1)}, bf16[2048,672]{0,1:T(8,128)(2,1)}, u32[]{:S(2)}, u32[]{:S(2)}) %collective-permute-start.10) | collective-permute-done | bytes 2752544 | tf_op jit(solution)/shard_map/ppermute | solution.py:154
  589.2 30.1 %collective-permute-done.9 = bf16[2048,672]{0,1:T(8,128)(2,1)} collective-permute-done((bf16[2048,672]{0,1:T(8,128)(2,1)}, bf16[2048,672]{0,1:T(8,128)(2,1)}, u32[]{:S(2)}, u32[]{:S(2)}) %collective-permute-start.9) | collective-permute-done | bytes 2752544 | tf_op jit(solution)/shard_map/ppermute | solution.py:154
  619.3 9.9 %fusion.22 = bf16[672,2048]{1,0:T(8,128)(2,1)S(1)} fusion(bf16[2048,672]{0,1:T(8,128)(2,1)} %collective-permute-done.13, bf16[2048,672]{0,1:T(8,128)(2,1)} %collective-permute-done.12, bf16[2048,672]{0,1:T(8,128)(2,1)} %collective-permute-done.11, bf16[2048,672]{0,1:T(8,128)(2,1)} %collective-permute-done.10, bf16[2048,672]{0,1:T(8,128)(2,1)} %collective-permute-done.9, ...), kind=kLoop, calls=%fused_computation.43 | loop fusion | flops 23396352 | bytes 24772612 | tf_op jit(solution)/shard_map/transpose | solution.py:155
  (84 shorter events, 37.6 us)
Async XLA Ops:
  7.2 3.2 copy-start.12
  7.2 103.3 %all-gather.2.cloned.1.call-start = ((), (), s32[]{:S(2)}) async-start(), calls=%async_computation | async-start | bytes 6881280 | tf_op jit(solution)/shard_map/all_gather | solution.py:89
  110.5 7.4 %copy-start.13 = (bf16[512,5376]{0,1:T(8,128)(2,1)S(1)}, bf16[512,5376]{0,1:T(8,128)(2,1)}, u32[]{:S(2)}) copy-start(bf16[512,5376]{0,1:T(8,128)(2,1)} %all-gather.2.cloned.1.call-done) | copy-start | bytes 16515076
  110.5 19.8 %slice-start = ((s8[11010048]{0:T(1024)(128)(4,1)}), s8[4194304]{0:T(1024)(128)(4,1)S(1)}, s32[]{:S(2)}) async-start(s8[11010048]{0:T(1024)(128)(4,1)} %bitcast.90), calls=%async_computation.1 | async-start | bytes 8388608
  110.5 19.8 %slice-start.1 = ((s8[11010048]{0:T(1024)(128)(4,1)}), s8[4194304]{0:T(1024)(128)(4,1)S(1)}, s32[]{:S(2)}) async-start(s8[11010048]{0:T(1024)(128)(4,1)} %bitcast.90), calls=%async_computation.2 | async-start | bytes 8388608
  117.9 12.5 %slice-start.2 = ((s8[11010048]{0:T(1024)(128)(4,1)}), s8[2621440]{0:T(1024)(128)(4,1)S(1)}, s32[]{:S(2)}) async-start(s8[11010048]{0:T(1024)(128)(4,1)} %bitcast.90), calls=%async_computation.3 | async-start | bytes 5242880
  123.7 23.8 %collective-permute-start.1 = (bf16[2,512,512]{2,1,0:T(8,128)(2,1)S(1)}, bf16[2,512,512]{2,1,0:T(8,128)(2,1)}, u32[]{:S(2)}, u32[]{:S(2)}) collective-permute-start(bf16[2,512,512]{2,1,0:T(8,128)(2,1)S(1)} %pad_maximum_fusion.1), channel_id=1, source_target_pairs={{0,4},{4,8},{8,12},{12,16},{16,20},{20,24},{24,28},{1,5},{5,9},{9,... | collective-permute-start | bytes 3145736 | tf_op jit(solution)/shard_map/ppermute | solution.py:19
  127.2 35.0 %collective-permute-start = (bf16[2,512,512]{2,1,0:T(8,128)(2,1)S(1)}, bf16[2,512,512]{2,1,0:T(8,128)(2,1)}, u32[]{:S(2)}, u32[]{:S(2)}) collective-permute-start(bf16[2,512,512]{2,1,0:T(8,128)(2,1)S(1)} %pad_maximum_fusion.1), channel_id=1, source_target_pairs={{0,8},{4,12},{8,16},{12,20},{16,24},{20,28},{1,9},{5,13},{9,17},{1... | collective-permute-start | bytes 3145736 | tf_op jit(solution)/shard_map/ppermute | solution.py:19
  166.7 17.7 %copy-start.1 = (bf16[1536,4,128,1]{0,2,3,1:T(8,128)(2,1)}, bf16[1536,4,128,1]{0,2,3,1:T(8,128)(2,1)S(1)}, u32[]{:S(2)}) copy-start(bf16[1536,4,128,1]{0,2,3,1:T(8,128)(2,1)S(1)} %copy.63) | copy-start | bytes 4718596
  166.7 4.1 copy-start.3
  166.7 4.1 copy-start.11
  201.9 17.0 %copy-start.2 = (bf16[1536,4,128,1]{0,2,3,1:T(8,128)(2,1)S(1)}, bf16[1536,4,128,1]{0,2,3,1:T(8,128)(2,1)}, u32[]{:S(2)}) copy-start(bf16[1536,4,128,1]{0,2,3,1:T(8,128)(2,1)} %copy-done.1) | copy-start | bytes 4718596
  228.7 11.0 %copy-start = (f32[4,128,1536]{2,1,0:T(8,128)S(1)}, f32[4,128,1536]{2,1,0:T(8,128)}, u32[]{:S(2)}) copy-start(f32[4,128,1536]{2,1,0:T(8,128)} %fusion.13) | copy-start | bytes 9437188
  239.7 8.5 %slice-start.3 = ((s8[11010048]{0:T(1024)(128)(4,1)}), s8[2621440]{0:T(1024)(128)(4,1)S(1)}, s32[]{:S(2)}) async-start(s8[11010048]{0:T(1024)(128)(4,1)} %bitcast.92), calls=%async_computation.4 | async-start | bytes 5242880
  239.7 8.5 %slice-start.4 = ((s8[11010048]{0:T(1024)(128)(4,1)}), s8[4194304]{0:T(1024)(128)(4,1)S(1)}, s32[]{:S(2)}) async-start(s8[11010048]{0:T(1024)(128)(4,1)} %bitcast.92), calls=%async_computation.5 | async-start | bytes 8388608
  240.3 4.4 copy-start.10
  240.5 28.0 %collective-permute-start.3 = (bf16[2,512,512]{1,2,0:T(8,128)(2,1)S(1)}, bf16[2,512,512]{1,2,0:T(8,128)(2,1)S(1)}, u32[]{:S(2)}, u32[]{:S(2)}) collective-permute-start(bf16[2,512,512]{1,2,0:T(8,128)(2,1)S(1)} %get-tuple-element.20), channel_id=1, source_target_pairs={{8,0},{12,4},{16,8},{20,12},{24,16},{28,20},{9,1},{13,5},{17,9},{2... | collective-permute-start | bytes 3145736 | tf_op jit(solution)/shard_map/ppermute | solution.py:19
  242.7 29.5 %collective-permute-start.2 = (bf16[2,512,512]{1,2,0:T(8,128)(2,1)S(1)}, bf16[2,512,512]{1,2,0:T(8,128)(2,1)S(1)}, u32[]{:S(2)}, u32[]{:S(2)}) collective-permute-start(bf16[2,512,512]{1,2,0:T(8,128)(2,1)S(1)} %get-tuple-element.19), channel_id=1, source_target_pairs={{4,0},{8,4},{12,8},{16,12},{20,16},{24,20},{28,24},{5,1},{9,5},{13... | collective-permute-start | bytes 3145736 | tf_op jit(solution)/shard_map/ppermute | solution.py:19
  244.7 3.6 slice-start.5
  279.3 45.3 %collective-permute-start.6 = (bf16[512,1344]{0,1:T(8,128)(2,1)}, bf16[512,1344]{0,1:T(8,128)(2,1)S(1)}, u32[]{:S(2)}, u32[]{:S(2)}) collective-permute-start(bf16[512,1344]{0,1:T(8,128)(2,1)} %fusion.19), channel_id=1, source_target_pairs={{0,1},{1,2},{2,3},{3,0},{4,5},{5,6},{6,7},{7,4},{8,9},{9,10},{10,1... | collective-permute-start | bytes 4128776 | tf_op jit(solution)/shard_map/ppermute | solution.py:138
  301.4 13.7 %copy-start.5 = (f32[512,1344]{0,1:T(8,128)S(1)}, f32[512,1344]{0,1:T(8,128)}, u32[]{:S(2)}) copy-start(f32[512,1344]{0,1:T(8,128)} %fusion.27) | copy-start | bytes 8257540
  313.9 97.3 %collective-permute-start.13 = (bf16[2048,672]{0,1:T(8,128)(2,1)S(1)}, bf16[2048,672]{0,1:T(8,128)(2,1)}, u32[]{:S(2)}, u32[]{:S(2)}) collective-permute-start(bf16[2048,672]{0,1:T(8,128)(2,1)S(1)} %get-tuple-element.13), channel_id=1, source_target_pairs={{0,4},{4,8},{8,12},{12,16},{16,20},{20,24},{24,28},{28,0},{1,5},{5... | collective-permute-start | bytes 8257544 | tf_op jit(solution)/shard_map/ppermute | solution.py:154
  314.0 116.4 %collective-permute-start.12 = (bf16[2048,672]{0,1:T(8,128)(2,1)S(1)}, bf16[2048,672]{0,1:T(8,128)(2,1)}, u32[]{:S(2)}, u32[]{:S(2)}) collective-permute-start(bf16[2048,672]{0,1:T(8,128)(2,1)S(1)} %get-tuple-element.14), channel_id=1, source_target_pairs={{0,8},{4,12},{8,16},{12,20},{16,24},{20,28},{24,0},{28,4},{1,9},{5... | collective-permute-start | bytes 8257544 | tf_op jit(solution)/shard_map/ppermute | solution.py:154
  319.8 90.4 %collective-permute-start.5 = (bf16[512,1344]{0,1:T(8,128)(2,1)S(1)}, bf16[512,1344]{0,1:T(8,128)(2,1)S(1)}, u32[]{:S(2)}, u32[]{:S(2)}) collective-permute-start(bf16[512,1344]{0,1:T(8,128)(2,1)S(1)} %fusion.18), channel_id=1, source_target_pairs={{0,2},{1,3},{2,0},{3,1},{4,6},{5,7},{6,4},{7,5},{8,10},{9,11},{10,... | collective-permute-start | bytes 4128776 | tf_op jit(solution)/shard_map/ppermute | solution.py:138
  324.3 85.8 %collective-permute-start.4 = (bf16[512,1344]{0,1:T(8,128)(2,1)S(1)}, bf16[512,1344]{0,1:T(8,128)(2,1)S(1)}, u32[]{:S(2)}, u32[]{:S(2)}) collective-permute-start(bf16[512,1344]{0,1:T(8,128)(2,1)S(1)} %fusion.17), channel_id=1, source_target_pairs={{0,3},{1,0},{2,1},{3,2},{4,7},{5,4},{6,5},{7,6},{8,11},{9,8},{10,9... | collective-permute-start | bytes 4128776 | tf_op jit(solution)/shard_map/ppermute | solution.py:138
  324.6 115.6 %collective-permute-start.11 = (bf16[2048,672]{0,1:T(8,128)(2,1)}, bf16[2048,672]{0,1:T(8,128)(2,1)}, u32[]{:S(2)}, u32[]{:S(2)}) collective-permute-start(bf16[2048,672]{0,1:T(8,128)(2,1)} %get-tuple-element.15), channel_id=1, source_target_pairs={{0,12},{4,16},{8,20},{12,24},{16,28},{20,0},{24,4},{28,8},{1,13},{... | collective-permute-start | bytes 8257544 | tf_op jit(solution)/shard_map/ppermute | solution.py:154
  410.1 20.2 %copy-start.6 = (bf16[512,1344]{0,1:T(8,128)(2,1)}, bf16[512,1344]{0,1:T(8,128)(2,1)S(1)}, u32[]{:S(2)}) copy-start(bf16[512,1344]{0,1:T(8,128)(2,1)S(1)} %collective-permute-done.5) | copy-start | bytes 4128772
  410.1 179.0 %collective-permute-start.10 = (bf16[2048,672]{0,1:T(8,128)(2,1)}, bf16[2048,672]{0,1:T(8,128)(2,1)}, u32[]{:S(2)}, u32[]{:S(2)}) collective-permute-start(bf16[2048,672]{0,1:T(8,128)(2,1)} %get-tuple-element.16), channel_id=1, source_target_pairs={{0,16},{4,20},{8,24},{12,28},{16,0},{20,4},{24,8},{28,12},{1,17},{... | collective-permute-start | bytes 8257544 | tf_op jit(solution)/shard_map/ppermute | solution.py:154
  410.2 20.2 %copy-start.8 = (bf16[512,1344]{0,1:T(8,128)(2,1)}, bf16[512,1344]{0,1:T(8,128)(2,1)S(1)}, u32[]{:S(2)}) copy-start(bf16[512,1344]{0,1:T(8,128)(2,1)S(1)} %collective-permute-done.4) | copy-start | bytes 4128772
  410.2 209.2 %collective-permute-start.9 = (bf16[2048,672]{0,1:T(8,128)(2,1)}, bf16[2048,672]{0,1:T(8,128)(2,1)}, u32[]{:S(2)}, u32[]{:S(2)}) collective-permute-start(bf16[2048,672]{0,1:T(8,128)(2,1)} %get-tuple-element.17), channel_id=1, source_target_pairs={{0,20},{4,24},{8,28},{12,0},{16,4},{20,8},{24,12},{28,16},{1,21},{... | collective-permute-start | bytes 8257544 | tf_op jit(solution)/shard_map/ppermute | solution.py:154
  411.1 208.2 %collective-permute-start.8 = (bf16[2048,672]{0,1:T(8,128)(2,1)}, bf16[2048,672]{0,1:T(8,128)(2,1)}, u32[]{:S(2)}, u32[]{:S(2)}) collective-permute-start(bf16[2048,672]{0,1:T(8,128)(2,1)} %get-tuple-element.18), channel_id=1, source_target_pairs={{0,24},{4,28},{8,0},{12,4},{16,8},{20,12},{24,16},{28,20},{1,25},{... | collective-permute-start | bytes 8257544 | tf_op jit(solution)/shard_map/ppermute | solution.py:154
  430.4 188.9 %collective-permute-start.7 = (bf16[2048,672]{0,1:T(8,128)(2,1)}, bf16[2048,672]{0,1:T(8,128)(2,1)}, u32[]{:S(2)}, u32[]{:S(2)}) collective-permute-start(bf16[2048,672]{0,1:T(8,128)(2,1)} %get-tuple-element.12), channel_id=1, source_target_pairs={{0,28},{4,0},{8,4},{12,8},{16,12},{20,16},{24,20},{28,24},{1,29},{... | collective-permute-start | bytes 8257544 | tf_op jit(solution)/shard_map/ppermute | solution.py:154
  (3 other events, 7.4 us)
Sparse Core Ops, SparseCore 0:
  9.6 100.8 all-gather.1
where the time goes:
time: 646 us; the launch traced here: 639 us
  waiting for transfers between devices  421 us (65%)
  matrix products  124 us (19%)
  other arithmetic  32.4 us (5%)
  local copies, waits for them, and re-layouts  27.2 us (4%)
  starting transfers between devices  19 us (3%)
  between operations  14.9 us (2%)
    ppermute x7, waiting for transfers between devices, per_device(): weight_sum = weight_sum + lax.ppermute(sent, SEQ, pairs).astype(jnp.float32)  196 us
    all_gather x1, waiting for transfers between devices, per_device(): gathered = lax.all_gather(tokens, 'head', axis=1, tiled=True)  97.3 us
    ppermute x3, waiting for transfers between devices, per_device(): got = lax.ppermute(sent, 'head', pairs).astype(jnp.float32)  85.2 us
    ppermute x4, waiting for transfers between devices, passed_along(): return lax.ppermute(x, axis, pairs)  41.7 us
    dot_general x12, matrix products, contract_last(): lax.dot_general(left, right, (((1,), (1,)), ((), ())), preferred_element_...  34 us
    dot_general x1, matrix products, contract_first(): lax.dot_general(left, right, (((0,), (0,)), ((), ())), preferred_element_...  19.3 us
    dot_general x1, matrix products, attend(): jnp.einsum('akgd,ckd->kgac', grad_four, value_three, preferred_element_ty...  17.5 us
    convert_element_type x1, other arithmetic, attend(): dscores = (probs * (dprobs - center)).astype(jnp.bfloat16)  17 us
  transfers between devices with their start and end apart: 15, of which 9 were waited for; matrix products, arithmetic and copies ran while one was open for 11% of the time, Pallas kernels for 0%

commit v1 on v0

--- a/solution.py
+++ b/solution.py
@@ -86,7 +86,13 @@
     tok_rows = tokens.shape[0]
     hop_count = HOPS
     margin = hop_count * tok_rows
-    gathered = lax.all_gather(tokens, "head", axis=1, tiled=True)
+    n_dev = lax.axis_size("head")
+    current, parts = (tokens, [tokens])
+    for _ in range(n_dev - 1):
+        current = lax.ppermute(current, "head", [(i_2, (i_2 + 1) % n_dev) for i_2 in range(n_dev)])
+        parts.insert(0, current)
+    row_of_blocks = jnp.concatenate(parts, axis=1)
+    gathered = jnp.roll(row_of_blocks, (lax.axis_index("head") + 1) * tokens.shape[1], axis=1)
     queries = jnp.dot(gathered, query_weight, preferred_element_type=jnp.float32).astype(
         jnp.bfloat16
     )

time: 646 us -> 623 us (0.964)
  waiting for transfers between devices: 421 us -> 401 us
  between operations: 14.9 us -> 1.69 us
  starting transfers between devices: 19 us -> 29.7 us
  local copies, waits for them, and re-layouts: 27.2 us -> 34.8 us
  matrix products: 124 us -> 117 us
    all_gather x1 -> x0, waiting for transfers between devices: 97.3 us -> none  [per_device(): gathered = lax.all_gather(tokens, 'head', axis=1, tiled=True)]
    ppermute x0 -> x3, waiting for transfers between devices: none -> 80.1 us  [per_device(): lax.ppermute(current, 'head', [(i_2, (i_2 + 1) % n_dev) for i_2 in range(...]
  transfers between devices with their start and end apart: 15 -> 17, of which waited for: 9 -> 11; matrix products, arithmetic and copies ran while one was open for 11% -> 12% of each run, Pallas kernels for 0% -> 0%
where the time goes in v1:
time: 623 us; the launch traced here: 616 us
  waiting for transfers between devices  401 us (64%)
  matrix products  117 us (19%)
  local copies, waits for them, and re-layouts  34.8 us (6%)
  other arithmetic  33.1 us (5%)
  starting transfers between devices  29.7 us (5%)
    ppermute x7, waiting for transfers between devices, per_device(): weight_sum = weight_sum + lax.ppermute(sent, SEQ, pairs).astype(jnp.float32)  196 us
    ppermute x3, waiting for transfers between devices, per_device(): got = lax.ppermute(sent, 'head', pairs).astype(jnp.float32)  84.5 us
    ppermute x3, waiting for transfers between devices, per_device(): lax.ppermute(current, 'head', [(i_2, (i_2 + 1) % n_dev) for i_2 in range(...  80.1 us
    ppermute x4, waiting for transfers between devices, passed_along(): return lax.ppermute(x, axis, pairs)  40 us
    dot_general x12, matrix products, contract_last(): lax.dot_general(left, right, (((1,), (1,)), ((), ())), preferred_element_...  34 us
    dot_general x1, matrix products, contract_first(): lax.dot_general(left, right, (((0,), (0,)), ((), ())), preferred_element_...  18.2 us
    dot_general x1, matrix products, attend(): jnp.einsum('akgd,ckd->kgac', grad_four, value_three, preferred_element_ty...  17.8 us
    convert_element_type x1, other arithmetic, attend(): dscores = (probs * (dprobs - center)).astype(jnp.bfloat16)  17 us
  transfers between devices with their start and end apart: 17, of which 11 were waited for; matrix products, arithmetic and copies ran while one was open for 12% of the time, Pallas kernels for 0%

profile of v1, /device:TPU:27, one launch (start us, length us, event | category | flops | bytes accessed | tf_op | source)
XLA Modules:
  0.0 616.4 jit_solution(6274446812092865056)
XLA Ops:
  0.7 31.2 %collective-permute-done = bf16[512,1344]{0,1:T(8,128)(2,1)S(1)} collective-permute-done((bf16[512,1344]{0,1:T(8,128)(2,1)}, bf16[512,1344]{0,1:T(8,128)(2,1)S(1)}, u32[]{:S(2)}, u32[]{:S(2)}) %collective-permute-start) | collective-permute-done | bytes 1376288 | tf_op jit(solution)/shard_map/ppermute | solution.py:92
  33.8 28.2 %collective-permute-done.1 = bf16[512,1344]{0,1:T(8,128)(2,1)S(1)} collective-permute-done((bf16[512,1344]{0,1:T(8,128)(2,1)S(1)}, bf16[512,1344]{0,1:T(8,128)(2,1)S(1)}, u32[]{:S(2)}, u32[]{:S(2)}) %collective-permute-start.1) | collective-permute-done | bytes 1376288 | tf_op jit(solution)/shard_map/ppermute | solution.py:92
  62.1 3.8 collective-permute-start.2
  72.3 20.6 %collective-permute-done.2 = bf16[512,1344]{0,1:T(8,128)(2,1)} collective-permute-done((bf16[512,1344]{0,1:T(8,128)(2,1)S(1)}, bf16[512,1344]{0,1:T(8,128)(2,1)}, u32[]{:S(2)}, u32[]{:S(2)}) %collective-permute-start.2) | collective-permute-done | bytes 1376288 | tf_op jit(solution)/shard_map/ppermute | solution.py:92
  102.0 3.0 fusion.71
  105.2 6.6 %collective-permute-start.4 = (bf16[2,512,512]{2,1,0:T(8,128)(2,1)S(1)}, bf16[2,512,512]{2,1,0:T(8,128)(2,1)}, u32[]{:S(2)}, u32[]{:S(2)}) collective-permute-start(bf16[2,512,512]{2,1,0:T(8,128)(2,1)S(1)} %pad_maximum_fusion.1), channel_id=1, source_target_pairs={{0,4},{4,8},{8,12},{12,16},{16,20},{20,24},{24,28},{1,5},{5,9},{9,... | collective-permute-start | bytes 3145736 | tf_op jit(solution)/shard_map/ppermute | solution.py:19
  111.8 3.6 collective-permute-start.3
  115.5 5.9 fusion.49
  124.3 7.8 %collective-permute-done.4 = bf16[2,512,512]{2,1,0:T(8,128)(2,1)} collective-permute-done((bf16[2,512,512]{2,1,0:T(8,128)(2,1)S(1)}, bf16[2,512,512]{2,1,0:T(8,128)(2,1)}, u32[]{:S(2)}, u32[]{:S(2)}) %collective-permute-start.4) | collective-permute-done | bytes 1048608 | tf_op jit(solution)/shard_map/ppermute | solution.py:19
  132.1 14.6 %collective-permute-done.3 = bf16[2,512,512]{2,1,0:T(8,128)(2,1)} collective-permute-done((bf16[2,512,512]{2,1,0:T(8,128)(2,1)S(1)}, bf16[2,512,512]{2,1,0:T(8,128)(2,1)}, u32[]{:S(2)}, u32[]{:S(2)}) %collective-permute-start.3) | collective-permute-done | bytes 1048608 | tf_op jit(solution)/shard_map/ppermute | solution.py:19
  151.3 4.0 reshape_squeeze.7
  155.3 13.6 %fusion.96 = (f32[4,2,512]{2,1,0:T(2,128)S(1)}, f32[4,2,512,1536]{2,3,1,0:T(8,128)}) fusion(pred[512,1536]{0,1:T(8,128)(4,1)S(1)} %copy-done.12, bf16[1536,4,128,1]{0,2,3,1:T(8,128)(2,1)S(1)} %copy.63, bf16[512,4,2,128]{0,3,2,1:T(8,128)(2,1)S(1)} %bitcast.81), kind=kOutput, calls=%fused_computation.129 | convolution fusion | flops 1642071552 | bytes 28590080 | tf_op jit(solution)/shard_map/sub | solution.py:59
  168.9 17.8 %fusion.1 = (f32[4,2,512]{2,1,0:T(2,128)S(1)}, f32[4,1536,512,2]{2,1,3,0:T(8,128)}) fusion(f32[4,2,512,1536]{2,3,1,0:T(8,128)} %get-tuple-element.28, f32[4,2,512]{2,1,0:T(2,128)S(1)} %get-tuple-element.27, bf16[512,4,2,128]{0,3,2,1:T(8,128)(2,1)} %bitcast.83, bf16[1536,4,128,1]{2,1,0,3:T(4,128)(2,1)} %bitcast.82), kind=kOutput, calls=%fused_computation.3 | convolution fusion | flops 1629483008 | bytes 52985856 | tf_op jit(solution)/shard_map/akgd,ckd->kgac/dot_general | solution.py:61
  186.7 17.0 %fusion.3 = bf16[4,2,512,1536]{2,3,1,0:T(8,128)(2,1)S(1)} fusion(f32[4,1536,512,2]{2,1,3,0:T(8,128)} %get-tuple-element.30, f32[4,2,512]{2,1,0:T(2,128)S(1)} %get-tuple-element.29, f32[4,2,512,1536]{2,3,1,0:T(8,128)} %get-tuple-element.28, f32[4,2,512]{2,1,0:T(2,128)S(1)} %get-tuple-element.27), kind=kLoop, calls=%fused_computation.5 | loop fusion | flops 25165824 | bytes 62947328 | tf_op jit(solution)/shard_map/convert_element_type | solution.py:65
  206.6 7.0 %fusion.20 = f32[4,128,1536]{2,1,0:T(8,128)} fusion(bf16[512,4,2,128]{0,3,2,1:T(8,128)(2,1)} %bitcast.80, bf16[4,2,512,1536]{2,3,1,0:T(8,128)(2,1)S(1)} %fusion.3), kind=kOutput, calls=%fused_computation.40 | convolution fusion | flops 1611399168 | bytes 16777216 | tf_op jit(solution)/shard_map/kgac,akgd->ckd/dot_general | solution.py:76
  213.5 11.0 %fusion.5 = f32[4,1536,128,1]{1,2,3,0:T(8,128)S(1)} fusion(bf16[512,4,2,128]{0,3,2,1:T(8,128)(2,1)} %bitcast.84, f32[4,2,512,1536]{2,3,1,0:T(8,128)} %get-tuple-element.28, f32[4,2,512]{2,1,0:T(2,128)S(1)} %get-tuple-element.27), kind=kOutput, calls=%fused_computation.10 | convolution fusion | flops 1623195648 | bytes 29376512 | tf_op jit(solution)/shard_map/kgac,akgd->ckd/dot_general | solution.py:79
  229.6 3.5 fusion.32
  233.1 3.2 fusion.34
  236.3 3.2 fusion.36
  239.5 13.9 %collective-permute-done.6 = bf16[2,512,512]{1,2,0:T(8,128)(2,1)S(1)} collective-permute-done((bf16[2,512,512]{1,2,0:T(8,128)(2,1)S(1)}, bf16[2,512,512]{1,2,0:T(8,128)(2,1)S(1)}, u32[]{:S(2)}, u32[]{:S(2)}) %collective-permute-start.6) | collective-permute-done | bytes 1048608 | tf_op jit(solution)/shard_map/ppermute | solution.py:19
  253.4 3.6 collective-permute-done.5
  260.8 3.3 fusion.26
  264.1 4.1 collective-permute-start.9
  268.2 18.2 %convolution_convert_fusion = bf16[2048,5376]{0,1:T(8,128)(2,1)} fusion(bf16[512,10752]{0,1:T(8,128)(2,1)} %copy-done.13, s32[]{:T(128)S(6)} %select_n.113, bf16[512,512]{0,1:T(8,128)(2,1)} %get-tuple-element.26, bf16[512,512]{0,1:T(8,128)(2,1)} %get-tuple-element.25, bf16[512,1024]{0,1:T(8,128)(2,1)S(1)} %bitcast.88), kind=kOutput, calls=%fused_computation.8 | convolution fusion | flops 11291590656 | bytes 29622276 | tf_op jit(solution)/shard_map/dot_general | solution.py:29
  286.4 12.4 %constant_dynamic-slice_fusion.6 = (bf16[2048,672]{0,1:T(8,128)(2,1)}, bf16[2048,672]{0,1:T(8,128)(2,1)S(1)}, bf16[2048,672]{0,1:T(8,128)(2,1)S(1)}, bf16[2048,6...) fusion(bf16[2048,5376]{0,1:T(8,128)(2,1)} %convolution_convert_fusion, ...), kind=kLoop, calls=%fused_computation.107 | loop fusion | bytes 38535196 | tf_op jit(solution)/shard_map/dynamic_slice | solution.py:154
  309.9 84.5 %collective-permute-done.8 = bf16[512,1344]{0,1:T(8,128)(2,1)S(1)} collective-permute-done((bf16[512,1344]{0,1:T(8,128)(2,1)S(1)}, bf16[512,1344]{0,1:T(8,128)(2,1)S(1)}, u32[]{:S(2)}, u32[]{:S(2)}) %collective-permute-start.8) | collective-permute-done | bytes 1376288 | tf_op jit(solution)/shard_map/ppermute | solution.py:144
  397.8 17.6 %collective-permute-done.15 = bf16[2048,672]{0,1:T(8,128)(2,1)} collective-permute-done((bf16[2048,672]{0,1:T(8,128)(2,1)S(1)}, bf16[2048,672]{0,1:T(8,128)(2,1)}, u32[]{:S(2)}, u32[]{:S(2)}) %collective-permute-start.15) | collective-permute-done | bytes 2752544 | tf_op jit(solution)/shard_map/ppermute | solution.py:160
  415.7 3.4 fusion.30
  421.5 3.7 add_convert_fusion
  425.2 148.3 %collective-permute-done.13 = bf16[2048,672]{0,1:T(8,128)(2,1)} collective-permute-done((bf16[2048,672]{0,1:T(8,128)(2,1)}, bf16[2048,672]{0,1:T(8,128)(2,1)}, u32[]{:S(2)}, u32[]{:S(2)}) %collective-permute-start.13) | collective-permute-done | bytes 2752544 | tf_op jit(solution)/shard_map/ppermute | solution.py:160
  573.5 30.1 %collective-permute-done.12 = bf16[2048,672]{0,1:T(8,128)(2,1)} collective-permute-done((bf16[2048,672]{0,1:T(8,128)(2,1)}, bf16[2048,672]{0,1:T(8,128)(2,1)}, u32[]{:S(2)}, u32[]{:S(2)}) %collective-permute-start.12) | collective-permute-done | bytes 2752544 | tf_op jit(solution)/shard_map/ppermute | solution.py:160
  603.6 9.9 %fusion.29 = bf16[672,2048]{1,0:T(8,128)(2,1)S(1)} fusion(bf16[2048,672]{0,1:T(8,128)(2,1)} %collective-permute-done.16, bf16[2048,672]{0,1:T(8,128)(2,1)} %collective-permute-done.15, bf16[2048,672]{0,1:T(8,128)(2,1)} %collective-permute-done.14, bf16[2048,672]{0,1:T(8,128)(2,1)} %collective-permute-done.13, bf16[2048,672]{0,1:T(8,128)(2,1)} %collective-permute-done.12, ...), kind=kLoop, calls=%fused_computation.50 | loop fusion | flops 23396352 | bytes 24772612 | tf_op jit(solution)/shard_map/transpose | solution.py:161
  (105 shorter events, 55.8 us)
Async XLA Ops:
  0.6 31.3 %collective-permute-start = (bf16[512,1344]{0,1:T(8,128)(2,1)}, bf16[512,1344]{0,1:T(8,128)(2,1)S(1)}, u32[]{:S(2)}, u32[]{:S(2)}) collective-permute-start(bf16[512,1344]{0,1:T(8,128)(2,1)} %param.6), channel_id=1, source_target_pairs={{0,1},{1,2},{2,3},{3,0},{4,5},{5,6},{6,7},{7,4},{8,9},{9,10},{10,1... | collective-permute-start | bytes 4128776 | tf_op jit(solution)/shard_map/ppermute | solution.py:92
  31.9 30.1 %collective-permute-start.1 = (bf16[512,1344]{0,1:T(8,128)(2,1)S(1)}, bf16[512,1344]{0,1:T(8,128)(2,1)S(1)}, u32[]{:S(2)}, u32[]{:S(2)}) collective-permute-start(bf16[512,1344]{0,1:T(8,128)(2,1)S(1)} %collective-permute-done), channel_id=1, source_target_pairs={{0,1},{1,2},{2,3},{3,0},{4,5},{5,6},{6,7},{7,4},{8,9},{9,10},{10,1... | collective-permute-start | bytes 4128776 | tf_op jit(solution)/shard_map/ppermute | solution.py:92
  62.1 30.8 %collective-permute-start.2 = (bf16[512,1344]{0,1:T(8,128)(2,1)S(1)}, bf16[512,1344]{0,1:T(8,128)(2,1)}, u32[]{:S(2)}, u32[]{:S(2)}) collective-permute-start(bf16[512,1344]{0,1:T(8,128)(2,1)S(1)} %collective-permute-done.1), channel_id=1, source_target_pairs={{0,1},{1,2},{2,3},{3,0},{4,5},{5,6},{6,7},{7,4},{8,9},{9,10},{10,1... | collective-permute-start | bytes 4128776 | tf_op jit(solution)/shard_map/ppermute | solution.py:92
  97.6 4.4 slice-start.2
  98.9 16.5 %copy-start.13 = (bf16[512,10752]{0,1:T(8,128)(2,1)}, bf16[512,10752]{0,1:T(8,128)(2,1)S(1)}, u32[]{:S(2)}) copy-start(bf16[512,10752]{0,1:T(8,128)(2,1)S(1)} %constant_dynamic-update-slice_fusion) | copy-start | bytes 33030148
  98.9 16.5 %slice-start.4 = ((s8[11010048]{0:T(1024)(128)(4,1)}), s8[4194304]{0:T(1024)(128)(4,1)S(1)}, s32[]{:S(2)}) async-start(s8[11010048]{0:T(1024)(128)(4,1)} %bitcast.90), calls=%async_computation.4 | async-start | bytes 8388608
  98.9 16.5 %slice-start.5 = ((s8[11010048]{0:T(1024)(128)(4,1)}), s8[4194304]{0:T(1024)(128)(4,1)S(1)}, s32[]{:S(2)}) async-start(s8[11010048]{0:T(1024)(128)(4,1)} %bitcast.90), calls=%async_computation.5 | async-start | bytes 8388608
  102.0 13.4 %slice-start.6 = ((s8[11010048]{0:T(1024)(128)(4,1)}), s8[2621440]{0:T(1024)(128)(4,1)S(1)}, s32[]{:S(2)}) async-start(s8[11010048]{0:T(1024)(128)(4,1)} %bitcast.90), calls=%async_computation.6 | async-start | bytes 5242880
  105.2 27.0 %collective-permute-start.4 = (bf16[2,512,512]{2,1,0:T(8,128)(2,1)S(1)}, bf16[2,512,512]{2,1,0:T(8,128)(2,1)}, u32[]{:S(2)}, u32[]{:S(2)}) collective-permute-start(bf16[2,512,512]{2,1,0:T(8,128)(2,1)S(1)} %pad_maximum_fusion.1), channel_id=1, source_target_pairs={{0,4},{4,8},{8,12},{12,16},{16,20},{20,24},{24,28},{1,5},{5,9},{9,... | collective-permute-start | bytes 3145736 | tf_op jit(solution)/shard_map/ppermute | solution.py:19
  111.8 35.0 %collective-permute-start.3 = (bf16[2,512,512]{2,1,0:T(8,128)(2,1)S(1)}, bf16[2,512,512]{2,1,0:T(8,128)(2,1)}, u32[]{:S(2)}, u32[]{:S(2)}) collective-permute-start(bf16[2,512,512]{2,1,0:T(8,128)(2,1)S(1)} %pad_maximum_fusion.1), channel_id=1, source_target_pairs={{0,8},{4,12},{8,16},{12,20},{16,24},{20,28},{1,9},{5,13},{9,17},{1... | collective-permute-start | bytes 3145736 | tf_op jit(solution)/shard_map/ppermute | solution.py:19
  151.3 17.6 %copy-start.1 = (bf16[1536,4,128,1]{0,2,3,1:T(8,128)(2,1)}, bf16[1536,4,128,1]{0,2,3,1:T(8,128)(2,1)S(1)}, u32[]{:S(2)}) copy-start(bf16[1536,4,128,1]{0,2,3,1:T(8,128)(2,1)S(1)} %copy.63) | copy-start | bytes 4718596
  151.3 4.1 copy-start.4
  186.7 17.0 %copy-start.2 = (bf16[1536,4,128,1]{0,2,3,1:T(8,128)(2,1)S(1)}, bf16[1536,4,128,1]{0,2,3,1:T(8,128)(2,1)}, u32[]{:S(2)}) copy-start(bf16[1536,4,128,1]{0,2,3,1:T(8,128)(2,1)} %copy-done.1) | copy-start | bytes 4718596
  213.5 11.0 %copy-start = (f32[4,128,1536]{2,1,0:T(8,128)S(1)}, f32[4,128,1536]{2,1,0:T(8,128)}, u32[]{:S(2)}) copy-start(f32[4,128,1536]{2,1,0:T(8,128)} %fusion.20) | copy-start | bytes 9437188
  224.6 8.5 %slice-start.7 = ((s8[11010048]{0:T(1024)(128)(4,1)}), s8[2621440]{0:T(1024)(128)(4,1)S(1)}, s32[]{:S(2)}) async-start(s8[11010048]{0:T(1024)(128)(4,1)} %bitcast.92), calls=%async_computation.7 | async-start | bytes 5242880
  224.6 8.5 %slice-start.8 = ((s8[11010048]{0:T(1024)(128)(4,1)}), s8[4194304]{0:T(1024)(128)(4,1)S(1)}, s32[]{:S(2)}) async-start(s8[11010048]{0:T(1024)(128)(4,1)} %bitcast.92), calls=%async_computation.8 | async-start | bytes 8388608
  225.2 4.4 copy-start.11
  225.4 28.0 %collective-permute-start.6 = (bf16[2,512,512]{1,2,0:T(8,128)(2,1)S(1)}, bf16[2,512,512]{1,2,0:T(8,128)(2,1)S(1)}, u32[]{:S(2)}, u32[]{:S(2)}) collective-permute-start(bf16[2,512,512]{1,2,0:T(8,128)(2,1)S(1)} %get-tuple-element.20), channel_id=1, source_target_pairs={{8,0},{12,4},{16,8},{20,12},{24,16},{28,20},{9,1},{13,5},{17,9},{2... | collective-permute-start | bytes 3145736 | tf_op jit(solution)/shard_map/ppermute | solution.py:19
  227.6 29.5 %collective-permute-start.5 = (bf16[2,512,512]{1,2,0:T(8,128)(2,1)S(1)}, bf16[2,512,512]{1,2,0:T(8,128)(2,1)S(1)}, u32[]{:S(2)}, u32[]{:S(2)}) collective-permute-start(bf16[2,512,512]{1,2,0:T(8,128)(2,1)S(1)} %get-tuple-element.19), channel_id=1, source_target_pairs={{4,0},{8,4},{12,8},{16,12},{20,16},{24,20},{28,24},{5,1},{9,5},{13... | collective-permute-start | bytes 3145736 | tf_op jit(solution)/shard_map/ppermute | solution.py:19
  264.1 45.5 %collective-permute-start.9 = (bf16[512,1344]{0,1:T(8,128)(2,1)}, bf16[512,1344]{0,1:T(8,128)(2,1)S(1)}, u32[]{:S(2)}, u32[]{:S(2)}) collective-permute-start(bf16[512,1344]{0,1:T(8,128)(2,1)} %fusion.26), channel_id=1, source_target_pairs={{0,1},{1,2},{2,3},{3,0},{4,5},{5,6},{6,7},{7,4},{8,9},{9,10},{10,1... | collective-permute-start | bytes 4128776 | tf_op jit(solution)/shard_map/ppermute | solution.py:144
  286.4 13.7 %copy-start.6 = (f32[512,1344]{0,1:T(8,128)S(1)}, f32[512,1344]{0,1:T(8,128)}, u32[]{:S(2)}) copy-start(f32[512,1344]{0,1:T(8,128)} %fusion.34) | copy-start | bytes 8257540
  298.9 96.6 %collective-permute-start.16 = (bf16[2048,672]{0,1:T(8,128)(2,1)S(1)}, bf16[2048,672]{0,1:T(8,128)(2,1)}, u32[]{:S(2)}, u32[]{:S(2)}) collective-permute-start(bf16[2048,672]{0,1:T(8,128)(2,1)S(1)} %get-tuple-element.13), channel_id=1, source_target_pairs={{0,4},{4,8},{8,12},{12,16},{16,20},{20,24},{24,28},{28,0},{1,5},{5... | collective-permute-start | bytes 8257544 | tf_op jit(solution)/shard_map/ppermute | solution.py:160
  299.0 116.4 %collective-permute-start.15 = (bf16[2048,672]{0,1:T(8,128)(2,1)S(1)}, bf16[2048,672]{0,1:T(8,128)(2,1)}, u32[]{:S(2)}, u32[]{:S(2)}) collective-permute-start(bf16[2048,672]{0,1:T(8,128)(2,1)S(1)} %get-tuple-element.14), channel_id=1, source_target_pairs={{0,8},{4,12},{8,16},{12,20},{16,24},{20,28},{24,0},{28,4},{1,9},{5... | collective-permute-start | bytes 8257544 | tf_op jit(solution)/shard_map/ppermute | solution.py:160
  304.8 89.6 %collective-permute-start.8 = (bf16[512,1344]{0,1:T(8,128)(2,1)S(1)}, bf16[512,1344]{0,1:T(8,128)(2,1)S(1)}, u32[]{:S(2)}, u32[]{:S(2)}) collective-permute-start(bf16[512,1344]{0,1:T(8,128)(2,1)S(1)} %fusion.25), channel_id=1, source_target_pairs={{0,2},{1,3},{2,0},{3,1},{4,6},{5,7},{6,4},{7,5},{8,10},{9,11},{10,... | collective-permute-start | bytes 4128776 | tf_op jit(solution)/shard_map/ppermute | solution.py:144
  309.4 85.1 %collective-permute-start.7 = (bf16[512,1344]{0,1:T(8,128)(2,1)S(1)}, bf16[512,1344]{0,1:T(8,128)(2,1)S(1)}, u32[]{:S(2)}, u32[]{:S(2)}) collective-permute-start(bf16[512,1344]{0,1:T(8,128)(2,1)S(1)} %fusion.24), channel_id=1, source_target_pairs={{0,3},{1,0},{2,1},{3,2},{4,7},{5,4},{6,5},{7,6},{8,11},{9,8},{10,9... | collective-permute-start | bytes 4128776 | tf_op jit(solution)/shard_map/ppermute | solution.py:144
  309.6 115.6 %collective-permute-start.14 = (bf16[2048,672]{0,1:T(8,128)(2,1)}, bf16[2048,672]{0,1:T(8,128)(2,1)}, u32[]{:S(2)}, u32[]{:S(2)}) collective-permute-start(bf16[2048,672]{0,1:T(8,128)(2,1)} %get-tuple-element.15), channel_id=1, source_target_pairs={{0,12},{4,16},{8,20},{12,24},{16,28},{20,0},{24,4},{28,8},{1,13},{... | collective-permute-start | bytes 8257544 | tf_op jit(solution)/shard_map/ppermute | solution.py:160
  394.5 20.9 %copy-start.7 = (bf16[512,1344]{0,1:T(8,128)(2,1)}, bf16[512,1344]{0,1:T(8,128)(2,1)S(1)}, u32[]{:S(2)}) copy-start(bf16[512,1344]{0,1:T(8,128)(2,1)S(1)} %collective-permute-done.8) | copy-start | bytes 4128772
  394.5 179.0 %collective-permute-start.13 = (bf16[2048,672]{0,1:T(8,128)(2,1)}, bf16[2048,672]{0,1:T(8,128)(2,1)}, u32[]{:S(2)}, u32[]{:S(2)}) collective-permute-start(bf16[2048,672]{0,1:T(8,128)(2,1)} %get-tuple-element.16), channel_id=1, source_target_pairs={{0,16},{4,20},{8,24},{12,28},{16,0},{20,4},{24,8},{28,12},{1,17},{... | collective-permute-start | bytes 8257544 | tf_op jit(solution)/shard_map/ppermute | solution.py:160
  394.5 20.9 %copy-start.9 = (bf16[512,1344]{0,1:T(8,128)(2,1)}, bf16[512,1344]{0,1:T(8,128)(2,1)S(1)}, u32[]{:S(2)}) copy-start(bf16[512,1344]{0,1:T(8,128)(2,1)S(1)} %collective-permute-done.7) | copy-start | bytes 4128772
  394.5 209.2 %collective-permute-start.12 = (bf16[2048,672]{0,1:T(8,128)(2,1)}, bf16[2048,672]{0,1:T(8,128)(2,1)}, u32[]{:S(2)}, u32[]{:S(2)}) collective-permute-start(bf16[2048,672]{0,1:T(8,128)(2,1)} %get-tuple-element.17), channel_id=1, source_target_pairs={{0,20},{4,24},{8,28},{12,0},{16,4},{20,8},{24,12},{28,16},{1,21},{... | collective-permute-start | bytes 8257544 | tf_op jit(solution)/shard_map/ppermute | solution.py:160
  395.4 208.2 %collective-permute-start.11 = (bf16[2048,672]{0,1:T(8,128)(2,1)}, bf16[2048,672]{0,1:T(8,128)(2,1)}, u32[]{:S(2)}, u32[]{:S(2)}) collective-permute-start(bf16[2048,672]{0,1:T(8,128)(2,1)} %get-tuple-element.18), channel_id=1, source_target_pairs={{0,24},{4,28},{8,0},{12,4},{16,8},{20,12},{24,16},{28,20},{1,25},{... | collective-permute-start | bytes 8257544 | tf_op jit(solution)/shard_map/ppermute | solution.py:160
  415.4 188.3 %collective-permute-start.10 = (bf16[2048,672]{0,1:T(8,128)(2,1)}, bf16[2048,672]{0,1:T(8,128)(2,1)}, u32[]{:S(2)}, u32[]{:S(2)}) collective-permute-start(bf16[2048,672]{0,1:T(8,128)(2,1)} %get-tuple-element.12), channel_id=1, source_target_pairs={{0,28},{4,0},{8,4},{12,8},{16,12},{20,16},{24,20},{28,24},{1,29},{... | collective-permute-start | bytes 8257544 | tf_op jit(solution)/shard_map/ppermute | solution.py:160
  (9 other events, 23.5 us)
